TPU v7x, 256 devices: a whole 4x4x8 slice. The times are simulated.
256 devices in a mesh: section: 2 (over core), seq: 32 (over z, x), cfg: 4 (over y).
Axes of the slice: x: 4, y: 4, z: 8, core: 2. Of those that a mesh axis runs over, the one named last changes fastest.
Arguments:
- hidden_states: bfloat16 [4, 4, 512, 3072], P('cfg', None, 'seq'), may hold values from -250 to 250
- latent: float32 [2, 4, 512, 64], P('section', None, 'seq'), may hold values from -6 to 6
- stale_cache: bfloat16 [2, 4, 32, 2048, 128], P('section', 'cfg', 'seq'), may hold values from -140 to 140
- qkv_weight: bfloat16 [2, 3072, 3, 2048], P('section', None, None, 'cfg'), may hold values from -0.109375 to 0.109375
- out_weight: bfloat16 [2, 3072, 2048], P('section', 'seq', 'cfg'), may hold values from -0.125 to 0.125
- modulation: float32 [2, 6, 3072], P('section'), may hold values from -2.5 to 2.5
- out_modulation: float32 [2, 3072], replicated, may hold values from -2.5 to 2.5
- proj_weight: bfloat16 [3072, 64], replicated, may hold values from -0.109375 to 0.109375
- solver_coef: float32 [2, 3], P('section'), may hold values from 0.5 to 2
- video_len: int32 [2], replicated, may hold values from 911 to 1822, as said below
- text_len: int32 [4], replicated, may hold values from 1 to 226, as said below
- positions: int32 [3, 2, 4, 512], P(None, None, None, 'seq'), may hold values from 0 to 47
Outputs:
- new_latent: float32 [2, 4, 512, 64], P('section', None, 'seq')
- new_cache: bfloat16 [2, 4, 32, 2048, 128], P('section', 'cfg', 'seq')
Inputs may be any that keep to these rules, and one draw needn't show every extreme that they name: `video_len`: in every draw one request has exactly 1822 video tokens. `text_len`: in every draw some sequence has all 226 text tokens live.
All inputs are finite; a program needn't handle non-finite values.
Results may differ from a plain program's by a relative error of at most 0.02.
Values may be sent and summed in bfloat16 or wider, within the bound.
No kernel may reach another device: no remote copies, remote signals or barrier semaphores. Data moves between devices by JAX's collectives and lax.ppermute only.
A program may use at most 128 MiB of HBM per device.

v0:
```python
import math
import jax
import jax.numpy as jnp
from jax import lax
from jax.sharding import PartitionSpec as P

HD = 64
TEXT = 226


def from_behind(value, axis, steps):
    count = lax.axis_size(axis)
    pairs = [(source, (source + steps) % count) for source in range(count)]
    return lax.ppermute(value, axis, pairs)


def row_norm(values):
    centered = values - jnp.mean(values, axis=-1, keepdims=True)
    return centered * lax.rsqrt(jnp.mean(centered * centered, axis=-1, keepdims=True) + 1e-05)


def head_norm(values):
    centered = values - jnp.mean(values, axis=-1, keepdims=True)
    return centered * lax.rsqrt(jnp.mean(centered * centered, axis=-1, keepdims=True) + 1e-06)


def rope_angles(places, head_size):
    half_size = head_size // 2
    pairs_t = head_size // 8
    pairs_h = (half_size - pairs_t) // 2
    pair_index = jnp.arange(half_size)
    first_part = pair_index < pairs_t
    second_part = jnp.logical_and(pair_index >= pairs_t, pair_index < pairs_t + pairs_h)
    third_part = pair_index >= pairs_t + pairs_h
    local_index = jnp.where(
        first_part,
        pair_index,
        jnp.where(second_part, pair_index - pairs_t, pair_index - pairs_t - pairs_h),
    )
    axis_span = jnp.where(first_part, 2 * pairs_t, 2 * pairs_h)
    frequency = jnp.exp(
        -math.log(10000.0) * 2.0 * local_index.astype(jnp.float32) / axis_span.astype(jnp.float32)
    )
    angles = places[0][..., None] * first_part.astype(jnp.float32)
    angles = angles + places[1][..., None] * second_part.astype(jnp.float32)
    angles = angles + places[2][..., None] * third_part.astype(jnp.float32)
    return angles * frequency


def rotate(values, cos_table, sin_table):
    half_size = values.shape[-1] // 2
    first_half = values[..., :half_size]
    second_half = values[..., half_size:]
    return jnp.concatenate(
        [
            first_half * cos_table - second_half * sin_table,
            second_half * cos_table + first_half * sin_table,
        ],
        axis=-1,
    )


def per_device(
    hidden_states,
    latent,
    stale_cache,
    qkv_weight,
    out_weight,
    modulation,
    out_modulation,
    proj_weight,
    solver_coef,
    video_len,
    text_len,
    positions,
):
    section_id = lax.axis_index("section")
    shard_id = lax.axis_index("seq")
    seq_devices = lax.axis_size("seq")
    cfg_devices = lax.axis_size("cfg")
    patches = hidden_states.shape[1]
    patch_dev = hidden_states.shape[2]
    width = hidden_states.shape[3]
    patch_len = patch_dev * seq_devices
    total_len = patch_len * patches
    group_heads = qkv_weight.shape[3] // HD
    seq_count = cfg_devices
    qkv_full = qkv_weight[0].reshape(width, 3, group_heads, HD)
    out_full = lax.all_gather(out_weight[0], "seq", axis=0, tiled=True).reshape(
        width, group_heads, HD
    )
    mod_rows = modulation[0]
    stale_rows = stale_cache[0, 0, 0]
    my_sequence = shard_id // group_heads
    row_ids = jnp.arange(total_len)
    text_limit = lax.dynamic_index_in_dim(text_len, my_sequence, keepdims=False)
    video_limit = lax.dynamic_index_in_dim(video_len, my_sequence // 2, keepdims=False)
    live_keys = jnp.where(row_ids < TEXT, row_ids < text_limit, row_ids - TEXT < video_limit)
    key_patch = row_ids // patch_len
    use_fresh = key_patch[None, :] <= jnp.arange(patches)[:, None]
    scale_factor = HD ** (-0.5)
    row_place = (
        jnp.arange(patches)[:, None] * patch_len
        + shard_id * patch_dev
        + jnp.arange(patch_dev)[None, :]
    )
    text_rows = (row_place < TEXT)[:, :, None]
    shift_rows = jnp.where(text_rows, mod_rows[3], mod_rows[0])
    scale_rows = jnp.where(text_rows, mod_rows[4], mod_rows[1])
    gate_rows = jnp.where(text_rows, mod_rows[5], mod_rows[2])
    angles = rope_angles(positions.astype(jnp.float32), HD)
    angles = jnp.where(text_rows[None], 0.0, angles)
    angles = jnp.repeat(angles, 2, axis=0)[:, None]
    cos_table = jnp.cos(angles)
    sin_table = jnp.sin(angles)

    def run(hidden):
        normed = row_norm(hidden.astype(jnp.float32))
        mixed_rows = (normed * (1.0 + scale_rows) + shift_rows).astype(jnp.bfloat16)
        mixed_rows = lax.all_gather(mixed_rows, "cfg", axis=0, tiled=True)
        projected = jnp.einsum(
            "spqd,djge->sgjpqe", mixed_rows, qkv_full, preferred_element_type=jnp.float32
        )
        queries = rotate(head_norm(projected[:, :, 0]), cos_table, sin_table)
        key_part = rotate(head_norm(projected[:, :, 1]), cos_table, sin_table)
        stacked = jnp.stack([queries, key_part, projected[:, :, 2]], axis=2).astype(jnp.bfloat16)
        outgoing = stacked.reshape(seq_count * group_heads, 3, patches, patch_dev * HD)
        incoming = lax.all_to_all(outgoing, "seq", split_axis=0, concat_axis=3, tiled=True)
        incoming = incoming.reshape(3, patches, patch_len, HD)
        fresh_rows = jnp.concatenate([incoming[1], incoming[2]], axis=-1).reshape(total_len, 2 * HD)
        key_rows = jnp.where(use_fresh[:, :, None], fresh_rows[None], stale_rows[None])
        scores = (
            jnp.einsum(
                "pqe,pke->pqk", incoming[0], key_rows[..., :HD], preferred_element_type=jnp.float32
            )
            * scale_factor
        )
        scores = jnp.where(live_keys[None, None, :], scores, -jnp.inf)
        row_max = jnp.max(scores, axis=-1, keepdims=True)
        weights = jnp.exp(scores - row_max)
        row_sum = jnp.sum(weights, axis=-1, keepdims=True)
        combined = jnp.einsum(
            "pqk,pke->pqe",
            weights.astype(jnp.bfloat16),
            key_rows[..., HD:],
            preferred_element_type=jnp.float32,
        )
        attended = (combined / row_sum).astype(jnp.bfloat16)
        attended = attended.reshape(patches, seq_devices, patch_dev * HD)[None]
        returned = lax.all_to_all(attended, "seq", split_axis=2, concat_axis=0, tiled=True)
        returned = returned.reshape(seq_count, group_heads, patches, patch_dev, HD)
        update = lax.psum_scatter(
            jnp.einsum("sgpqe,dge->spqd", returned, out_full, preferred_element_type=jnp.float32),
            "cfg",
            scatter_dimension=0,
            tiled=True,
        )
        result = (hidden.astype(jnp.float32) + gate_rows * update).astype(jnp.bfloat16)
        return (result, fresh_rows)

    first_out, first_cache = run(hidden_states)
    received = from_behind(first_out, "section", 1)
    second_out, second_cache = run(received)
    key_cache = jnp.where(section_id == 0, first_cache, second_cache)
    normed = row_norm(second_out.astype(jnp.float32))
    normed_out = (normed * (1.0 + out_modulation[1]) + out_modulation[0]).astype(jnp.bfloat16)
    predicted = jnp.einsum(
        "spqd,do->spqo", normed_out, proj_weight, preferred_element_type=jnp.float32
    )
    predicted_all = lax.all_gather(predicted, ("section", "cfg"), axis=0, tiled=True)
    predicted_all = predicted_all[predicted_all.shape[0] - seq_count :]
    pair_rows = lax.dynamic_slice_in_dim(predicted_all, 2 * section_id, 2, 0)
    solver_row = solver_coef[0]
    guided = pair_rows[0] + solver_row[2] * (pair_rows[1] - pair_rows[0])
    new_latent = solver_row[0] * latent[0] + solver_row[1] * guided
    return (new_latent[None], key_cache[None, None, None])


def solution(mesh):
    return jax.shard_map(
        per_device,
        mesh=mesh,
        in_specs=(
            P("cfg", None, "seq", None),
            P("section", None, "seq", None),
            P("section", "cfg", "seq", None, None),
            P("section", None, None, "cfg"),
            P("section", "seq", "cfg"),
            P("section", None, None),
            P(),
            P(),
            P("section", None),
            P(),
            P(),
            P(None, None, None, "seq"),
        ),
        out_specs=(P("section", None, "seq", None), P("section", "cfg", "seq", None, None)),
        check_vma=False,
    )
```

profile of v0, /device:TPU:1, one launch (start us, length us, event | category | flops | bytes accessed | tf_op | source)
XLA Modules:
  0.0 396.4 jit_solution(5097558336061669999)
XLA Ops:
  8.2 1.4 fusion.91
  9.6 1.1 convert_reduce_fusion.1
  10.7 1.2 fusion.52
  12.0 2.0 fusion.58
  14.1 12.7 %copy.39 = bf16[1,3072,3,512]{1,3,2,0:T(8,128)(2,1)} copy(bf16[1,3072,3,512]{3,1,2,0:T(8,128)(2,1)} %param.15) | data formatting | bytes 18874368 | tf_op args[3]
  27.2 19.9 %all-gather.6.cloned.1.call-done = bf16[4,4,16,3072]{3,2,1,0:T(8,128)(2,1)} async-done(((bf16[1,4,16,3072]{3,2,1,0:T(8,128)(2,1)}), bf16[4,4,16,3072]{3,2,1,0:T(8,128)(2,1)}) %all-gather.6.cloned.1.call-update) | async-done | bytes 1572880 | tf_op jit(solution)/shard_map/all_gather | solution.py:120
  47.1 8.1 %convolution_bitcast_fusion.3 = f32[4,8,3,4,16,64]{5,4,1,2,3,0:T(8,128)S(1)} fusion(bf16[3072,3,8,64,1,1]{0,3,2,1,5,4:T(8,128)(2,1)} %bitcast.167, bf16[4,4,16,3072]{3,2,1,0:T(8,128)(2,1)} %all-gather.6.cloned.1.call-done), kind=kOutput, calls=%fused_computation.19 | convolution fusion | flops 2415919104 | bytes 12582912 | tf_op jit(solution)/shard_map/spqd,djge->sgjpqe/dot_general | solution.py:121
  56.1 1.3 multiply_reduce_fusion.3
  57.4 1.3 fusion.43
  61.4 1.5 copy.44
  62.9 9.5 %all-to-all-start = ((bf16[32,3,4,1024]{3,2,1,0:T(4,128)(2,1)}), bf16[32,3,4,1024]{3,2,1,0:T(4,128)(2,1)S(1)}, u32[]{:S(2)}, u32[]{:S(2)}) async-start(bf16[32,3,4,1024]{3,2,1,0:T(4,128)(2,1)} %copy.44), calls=%async_computation | async-start | bytes 1572864 | tf_op jit(solution)/shard_map/all_to_all | solution.py:128
  73.6 1.2 copy.49
  76.0 1.2 fusion.78
  77.9 15.6 %all-to-all-done = bf16[32,3,4,1024]{3,2,1,0:T(4,128)(2,1)S(1)} async-done(((bf16[32,3,4,1024]{3,2,1,0:T(4,128)(2,1)}), bf16[32,3,4,1024]{3,2,1,0:T(4,128)(2,1)S(1)}, u32[]{:S(2)}, u32[]{:S(2)}) %all-to-all-start) | async-done | bytes 786464 | tf_op jit(solution)/shard_map/all_to_all | solution.py:128
  96.6 2.5 fusion
  99.2 3.7 fusion.2
  102.9 4.0 %fusion.25 = bf16[4,512,64]{1,2,0:T(8,128)(2,1)S(1)} fusion(bf16[4,2048,128]{1,2,0:T(8,128)(2,1)S(1)} %broadcast_select_fusion.1, f32[4,512,2048]{2,1,0:T(8,128)S(1)} %get-tuple-element.49, f32[4,512]{1,0:T(4,128)S(1)} %get-tuple-element.48, pred[2048]{0:T(1024)(128)(4,1)S(1)} %fusion.78, f32[4,512]{1,0:T(4,128)S(1)} %fusion.2), kind=kOutput, calls=%fused_computation.58 | convolution fusion | flops 553910272 | bytes 18106368 | tf_op jit(solution)/shard_map/pqk,pke->pqe/dot_general | solution.py:142
  107.8 16.0 %all_to_all.60 = bf16[1,4,32,1024]{3,1,0,2:T(4,128)(2,1)S(1)} all-to-all(bf16[1,4,32,1024]{3,1,0,2:T(4,128)(2,1)S(1)} %copy.52), channel_id=1, replica_groups=mesh['section'=2,'seq'=32,'cfg'=4] {'seq'}, dimensions={2} | all-to-all | bytes 524288 | tf_op jit(solution)/shard_map/all_to_all | solution.py:150
  124.3 27.8 %all-gather.10.cloned.1.call-done = bf16[1,3072,512]{2,1,0:T(8,128)(2,1)} async-done(((bf16[1,96,512]{2,1,0:T(8,128)(2,1)}), bf16[1,3072,512]{2,1,0:T(8,128)(2,1)}) %all-gather.10.cloned.1.call-update) | async-done | bytes 3145744 | tf_op jit(solution)/shard_map/all_gather | solution.py:89
  152.0 4.6 %copy.54 = bf16[1,3072,512]{1,2,0:T(8,128)(2,1)} copy(bf16[1,3072,512]{2,1,0:T(8,128)(2,1)} %all-gather.10.cloned.1.call-done) | data formatting | bytes 6291456 | tf_op jit(solution)/shard_map/all_gather | solution.py:89
  156.7 4.5 %convolution_bitcast_fusion.1 = f32[4,4,16,3072]{3,2,1,0:T(8,128)} fusion(bf16[4,8,4,16,64]{4,3,2,1,0:T(8,128)(2,1)S(1)} %reshape.453, bf16[3072,8,64,1,1]{0,2,4,1,3:T(8,128)(2,1)} %bitcast.169), kind=kOutput, calls=%fused_computation.15 | convolution fusion | flops 805306368 | bytes 6553600 | tf_op jit(solution)/shard_map/sgpqe,dge->spqd/dot_general | solution.py:153
  161.3 41.5 %reduce-scatter.3.cloned.1.call-done = f32[1,4,16,3072]{3,2,1,0:T(8,128)} async-done(((f32[4,4,16,3072]{3,2,1,0:T(8,128)}), f32[1,4,16,3072]{3,2,1,0:T(8,128)}) %reduce-scatter.3.cloned.1.call-update) | async-done | bytes 786448 | tf_op jit(solution)/shard_map/reduce_scatter | solution.py:152
  202.8 1.3 fusion.60
  204.9 1.3 collective-permute-done
  206.7 1.0 fusion.59
  207.9 28.5 %all-gather.8.cloned.1.call-done = bf16[4,4,16,3072]{3,2,1,0:T(8,128)(2,1)} async-done(((bf16[1,4,16,3072]{3,2,1,0:T(8,128)(2,1)}), bf16[4,4,16,3072]{3,2,1,0:T(8,128)(2,1)}) %all-gather.8.cloned.1.call-update) | async-done | bytes 1572880 | tf_op jit(solution)/shard_map/all_gather | solution.py:120
  236.4 8.1 %convolution_bitcast_fusion.2 = f32[4,8,3,4,16,64]{5,4,1,3,0,2:T(8,128)S(1)} fusion(bf16[3072,3,8,64,1,1]{0,3,2,5,4,1:T(8,128)(2,1)} %bitcast.168, bf16[4,4,16,3072]{3,2,1,0:T(8,128)(2,1)} %all-gather.8.cloned.1.call-done), kind=kOutput, calls=%fused_computation.18 | convolution fusion | flops 2415919104 | bytes 12582912 | tf_op jit(solution)/shard_map/spqd,djge->sgjpqe/dot_general | solution.py:121
  245.3 1.3 multiply_reduce_fusion.1
  246.7 1.3 fusion.41
  249.1 1.1 stack.26
  251.2 1.0 pad_maximum_fusion.1
  252.9 30.6 %all_to_all.61 = bf16[32,3,4,1024]{3,2,1,0:T(4,128)(2,1)S(1)} all-to-all(bf16[32,3,4,1024]{3,2,1,0:T(4,128)(2,1)S(1)} %copy.60), channel_id=1, replica_groups=mesh['section'=2,'seq'=32,'cfg'=4] {'seq'}, dimensions={0} | all-to-all | bytes 1572864 | tf_op jit(solution)/shard_map/all_to_all | solution.py:128
  283.5 1.0 fusion.89
  285.7 1.0 copy.64
  286.7 1.3 broadcast_select_fusion
  288.0 1.7 copy.61
  289.7 1.3 squeeze.83
  291.1 2.5 fusion.1
  293.6 3.7 fusion.4
  297.3 4.7 %fusion.35 = bf16[4,512,64]{1,2,0:T(8,128)(2,1)} fusion(bf16[4,2048,128]{1,2,0:T(8,128)(2,1)S(1)} %broadcast_select_fusion, f32[4,512,2048]{2,1,0:T(8,128)S(1)} %get-tuple-element.51, f32[4,512]{1,0:T(4,128)S(1)} %get-tuple-element.50, pred[2048]{0:T(1024)(128)(4,1)S(1)} %fusion.78, f32[4,512]{1,0:T(4,128)S(1)} %fusion.4), kind=kOutput, calls=%fused_computation.60 | convolution fusion | flops 553910272 | bytes 18106368 | tf_op jit(solution)/shard_map/pqk,pke->pqe/dot_general | solution.py:142
  302.0 1.3 copy.66
  303.9 16.0 %all_to_all.62 = bf16[1,4,32,1024]{3,1,0,2:T(4,128)(2,1)S(1)} all-to-all(bf16[1,4,32,1024]{3,1,0,2:T(4,128)(2,1)S(1)} %copy.67), channel_id=1, replica_groups=mesh['section'=2,'seq'=32,'cfg'=4] {'seq'}, dimensions={2} | all-to-all | bytes 524288 | tf_op jit(solution)/shard_map/all_to_all | solution.py:150
  320.2 4.6 %convolution_bitcast_fusion = f32[4,4,16,3072]{3,2,1,0:T(8,128)} fusion(bf16[4,8,4,16,64]{4,3,2,1,0:T(8,128)(2,1)S(1)} %reshape.454, bf16[3072,8,64,1,1]{0,2,4,1,3:T(8,128)(2,1)} %bitcast.170), kind=kOutput, calls=%fused_computation.14 | convolution fusion | flops 805306368 | bytes 6553600 | tf_op jit(solution)/shard_map/sgpqe,dge->spqd/dot_general | solution.py:153
  327.0 1.4 maximum_select_fusion
  328.3 34.1 %reduce-scatter.5.cloned.1.call-done = f32[1,4,16,3072]{3,2,1,0:T(8,128)} async-done(((f32[4,4,16,3072]{3,2,1,0:T(8,128)}), f32[1,4,16,3072]{3,2,1,0:T(8,128)}) %reduce-scatter.5.cloned.1.call-update) | async-done | bytes 786448 | tf_op jit(solution)/shard_map/reduce_scatter | solution.py:152
  362.4 1.4 convert_reduce_fusion.2
  364.5 22.1 %all-gather.1 = f32[32,16,64]{2,1,0:T(8,128)S(1)} all-gather(f32[4,16,64]{2,1,0:T(8,128)S(1)} %fusion.63), channel_id=3, replica_groups=mesh['section'=2,'seq'=32,'cfg'=4] {'section','cfg'}, dimensions={0}, use_global_device_ids=true | all-gather | bytes 147456 | tf_op jit(solution)/shard_map/all_gather | solution.py:170
  386.6 2.5 fusion.75
  (151 shorter events, 20.8 us)
Async XLA Ops:
  8.0 356.1 %copy-start = (bf16[3072,64]{0,1:T(8,128)(2,1)S(1)}, bf16[3072,64]{0,1:T(8,128)(2,1)}, u32[]{:S(2)}) copy-start(bf16[3072,64]{0,1:T(8,128)(2,1)} %param.19) | copy-start | bytes 1179652
  8.0 39.1 %all-gather.6.cloned.1.call-start = ((), (), s32[]{:S(2)}) async-start(), calls=%async_computation.6 | async-start | bytes 1966080 | tf_op jit(solution)/shard_map/all_gather | solution.py:120
  8.1 18.7 %copy-start.22 = (pred[4,16]{1,0:T(4,128)(4,1)}, pred[4,16]{1,0:T(4,128)(4,1)S(1)}, u32[]{:S(2)}) copy-start(pred[4,16]{1,0:T(4,128)(4,1)S(1)} %add_compare_fusion.1) | copy-start | bytes 196
  9.5 2.4 copy-start.11
  9.6 2.4 copy-start.13
  9.6 2.4 copy-start.15
  9.6 2.4 copy-start.17
  14.1 12.7 %copy-start.24 = (s32[3,2,4,16]{3,2,1,0:T(4,128)S(1)}, s32[3,2,4,16]{3,2,1,0:T(4,128)}, u32[]{:S(2)}) copy-start(s32[3,2,4,16]{3,2,1,0:T(4,128)} %param.23) | copy-start | bytes 4612
  59.5 15.3 %copy-start.26 = (s32[2]{0:T(128)S(1)}, s32[2]{0:T(128)}, u32[]{:S(2)}) copy-start(s32[2]{0:T(128)} %param.21) | copy-start | bytes 28
  59.5 15.9 %copy-start.27 = (s32[4]{0:T(128)S(1)}, s32[4]{0:T(128)}, u32[]{:S(2)}) copy-start(s32[4]{0:T(128)} %param.22) | copy-start | bytes 52
  62.9 30.6 %all-to-all-start = ((bf16[32,3,4,1024]{3,2,1,0:T(4,128)(2,1)}), bf16[32,3,4,1024]{3,2,1,0:T(4,128)(2,1)S(1)}, u32[]{:S(2)}, u32[]{:S(2)}) async-start(bf16[32,3,4,1024]{3,2,1,0:T(4,128)(2,1)} %copy.44), calls=%async_computation | async-start | bytes 1572864 | tf_op jit(solution)/shard_map/all_to_all | solution.py:128
  72.4 79.6 %all-gather.10.cloned.1.call-start = ((), (), s32[]{:S(2)}) async-start(), calls=%async_computation.10 | async-start | bytes 3244032 | tf_op jit(solution)/shard_map/all_gather | solution.py:89
  73.0 129.8 %reduce-scatter.3.cloned.1.call-start = ((), (), s32[]{:S(2)}) async-start(), calls=%async_computation.7 | async-start | bytes 3932160 | tf_op jit(solution)/shard_map/reduce_scatter | solution.py:152
  93.9 1.3 copy-start.2
  94.3 0.9 copy-start.4
  124.2 78.7 %copy-start.1 = (bf16[1,4,16,3072]{3,2,1,0:T(8,128)(2,1)S(1)}, bf16[1,4,16,3072]{3,2,1,0:T(8,128)(2,1)}, u32[]{:S(2)}) copy-start(bf16[1,4,16,3072]{3,2,1,0:T(8,128)(2,1)} %param.12) | copy-start | bytes 1179652
  124.2 78.6 %copy-start.10 = (f32[1,1,3072]{2,0,1:T(1,128)S(1)}, f32[1,1,3072]{2,0,1:T(1,128)}, u32[]{:S(2)}) copy-start(f32[1,1,3072]{2,0,1:T(1,128)} %get-tuple-element.35) | copy-start | bytes 36868
  124.2 78.6 %copy-start.23 = (pred[4,16]{1,0:T(4,128)(4,1)S(1)}, pred[4,16]{1,0:T(4,128)(4,1)}, u32[]{:S(2)}) copy-start(pred[4,16]{1,0:T(4,128)(4,1)} %copy-done.22) | copy-start | bytes 196
  124.2 82.4 %copy-start.12 = (f32[1,1,3072]{2,0,1:T(1,128)S(1)}, f32[1,1,3072]{2,0,1:T(1,128)}, u32[]{:S(2)}) copy-start(f32[1,1,3072]{2,0,1:T(1,128)} %copy-done.11) | copy-start | bytes 36868
  124.2 82.4 %copy-start.14 = (f32[1,1,3072]{2,0,1:T(1,128)S(1)}, f32[1,1,3072]{2,0,1:T(1,128)}, u32[]{:S(2)}) copy-start(f32[1,1,3072]{2,0,1:T(1,128)} %copy-done.13) | copy-start | bytes 36868
  124.2 82.4 %copy-start.16 = (f32[1,1,3072]{2,0,1:T(1,128)S(1)}, f32[1,1,3072]{2,0,1:T(1,128)}, u32[]{:S(2)}) copy-start(f32[1,1,3072]{2,0,1:T(1,128)} %copy-done.15) | copy-start | bytes 36868
  124.2 82.4 %copy-start.18 = (f32[1,1,3072]{2,0,1:T(1,128)S(1)}, f32[1,1,3072]{2,0,1:T(1,128)}, u32[]{:S(2)}) copy-start(f32[1,1,3072]{2,0,1:T(1,128)} %copy-done.17) | copy-start | bytes 36868
  161.2 75.2 %all-gather.8.cloned.1.call-start = ((), (), s32[]{:S(2)}) async-start(), calls=%async_computation.8 | async-start | bytes 1966080 | tf_op jit(solution)/shard_map/all_gather | solution.py:120
  204.2 2.1 collective-permute-start
  207.7 154.7 %reduce-scatter.5.cloned.1.call-start = ((), (), s32[]{:S(2)}) async-start(), calls=%async_computation.9 | async-start | bytes 3932160 | tf_op jit(solution)/shard_map/reduce_scatter | solution.py:152
  250.1 36.6 %copy-start.19 = (pred[4,2048]{1,0:T(4,128)(4,1)S(1)}, pred[4,2048]{1,0:T(4,128)(4,1)}, u32[]{:S(2)}) copy-start(pred[4,2048]{1,0:T(4,128)(4,1)} %iota_compare_fusion) | copy-start | bytes 24580
  284.6 1.1 copy-start.6
  284.6 1.0 copy-start.8
  302.0 22.9 %copy-start.25 = (f32[1,3]{1,0:T(1,128)S(1)}, f32[1,3]{1,0:T(1,128)}, u32[]{:S(2)}) copy-start(f32[1,3]{1,0:T(1,128)} %param.20) | copy-start | bytes 40
  302.0 23.5 %copy-start.21 = (f32[2,3072]{1,0:T(2,128)S(1)}, f32[2,3072]{1,0:T(2,128)}, u32[]{:S(2)}) copy-start(f32[2,3072]{1,0:T(2,128)} %param.18) | copy-start | bytes 73732
  302.0 23.5 %copy-start.3 = (bf16[1,1,4,32,1024]{4,3,2,1,0:T(8,128)(2,1)S(1)}, bf16[1,1,4,32,1024]{4,3,2,1,0:T(8,128)(2,1)}, u32[]{:S(2)}) copy-start(bf16[1,1,4,32,1024]{4,3,2,1,0:T(8,128)(2,1)} %copy-done.2) | copy-start | bytes 786436
  302.0 23.9 %copy-start.5 = (bf16[1,1,4,32,1024]{4,3,2,1,0:T(8,128)(2,1)S(1)}, bf16[1,1,4,32,1024]{4,3,2,1,0:T(8,128)(2,1)}, u32[]{:S(2)}) copy-start(bf16[1,1,4,32,1024]{4,3,2,1,0:T(8,128)(2,1)} %copy-done.4) | copy-start | bytes 786436
  302.0 24.3 %copy-start.7 = (bf16[1,1,4,32,1024]{4,3,2,1,0:T(8,128)(2,1)S(1)}, bf16[1,1,4,32,1024]{4,3,2,1,0:T(8,128)(2,1)}, u32[]{:S(2)}) copy-start(bf16[1,1,4,32,1024]{4,3,2,1,0:T(8,128)(2,1)} %copy-done.6) | copy-start | bytes 786436
  302.0 24.6 %copy-start.9 = (bf16[1,1,4,32,1024]{4,3,2,1,0:T(8,128)(2,1)S(1)}, bf16[1,1,4,32,1024]{4,3,2,1,0:T(8,128)(2,1)}, u32[]{:S(2)}) copy-start(bf16[1,1,4,32,1024]{4,3,2,1,0:T(8,128)(2,1)} %copy-done.8) | copy-start | bytes 786436
  324.8 61.8 %copy-start.20 = (f32[1,4,16,64]{3,2,1,0:T(8,128)S(1)}, f32[1,4,16,64]{3,2,1,0:T(8,128)}, u32[]{:S(2)}) copy-start(f32[1,4,16,64]{3,2,1,0:T(8,128)} %param.13) | copy-start | bytes 49156
Sparse Core Ops, SparseCore 0:
  14.2 32.8 all-gather.5
  161.4 41.4 reduce-scatter.2
  207.8 28.5 all-gather.7
  324.9 37.3 reduce-scatter.4
Sparse Core Ops, SparseCore 1:
  75.5 76.5 all-gather.9
where the time goes:
time: 404 us; the launch traced here: 396 us
  waiting for transfers between devices  169 us (42%)
  blocking collectives  84.7 us (21%)
  local copies, waits for them, and re-layouts  39.7 us (10%)
  matrix products  39.5 us (10%)
  other arithmetic  35.8 us (9%)
  between operations  16.5 us (4%)
  starting transfers between devices  11.1 us (3%)
    reduce_scatter x2, waiting for transfers between devices, run(): lax.psum_scatter(jnp.einsum('sgpqe,dge->spqd', returned, out_full, prefer...  75.6 us
    all_gather x2, waiting for transfers between devices, run(): mixed_rows = lax.all_gather(mixed_rows, 'cfg', axis=0, tiled=True)  48.4 us
    all_to_all x2, blocking collectives, run(): lax.all_to_all(attended, 'seq', split_axis=2, concat_axis=0, tiled=True)  32 us
    all_to_all x1, blocking collectives, run(): lax.all_to_all(outgoing, 'seq', split_axis=0, concat_axis=3, tiled=True)  30.6 us
    all_gather x1, waiting for transfers between devices, per_device(): lax.all_gather(out_weight[0], 'seq', axis=0, tiled=True)  27.8 us
    all_gather x1, blocking collectives, per_device(): lax.all_gather(predicted, ('section', 'cfg'), axis=0, tiled=True)  22.1 us
    dot_general x2, matrix products, run(): jnp.einsum('spqd,djge->sgjpqe', mixed_rows, qkv_full, preferred_element_t...  16.2 us
    all_to_all x1, waiting for transfers between devices, run(): lax.all_to_all(outgoing, 'seq', split_axis=0, concat_axis=3, tiled=True)  15.6 us
  transfers between devices with their start and end apart: 7, of which 7 were waited for; matrix products, arithmetic and copies ran while one was open for 9% of the time, Pallas kernels for 0%

commit v1 on v0

--- a/solution.py
+++ b/solution.py
@@ -86,9 +86,9 @@
     group_heads = qkv_weight.shape[3] // HD
     seq_count = cfg_devices
     qkv_full = qkv_weight[0].reshape(width, 3, group_heads, HD)
-    out_full = lax.all_gather(out_weight[0], "seq", axis=0, tiled=True).reshape(
-        width, group_heads, HD
-    )
+    out_full = jnp.concatenate(
+        lax.all_to_all(jnp.stack([out_weight[0]] * lax.axis_size("seq")), "seq", 0, 0), axis=0
+    ).reshape(width, group_heads, HD)
     mod_rows = modulation[0]
     stale_rows = stale_cache[0, 0, 0]
     my_sequence = shard_id // group_heads

time: 404 us -> 459 us (1.14)
  waiting for transfers between devices: 169 us -> 210 us
  local copies, waits for them, and re-layouts: 39.7 us -> 53 us
    all_to_all x0 -> x1, waiting for transfers between devices: none -> 66.6 us  [per_device(): lax.all_to_all(jnp.stack([out_weight[0]] * lax.axis_size('seq')), 'seq',...]
    all_gather x1 -> x0, waiting for transfers between devices: 27.8 us -> none  [per_device(): lax.all_gather(out_weight[0], 'seq', axis=0, tiled=True)]
    another operation x0 -> x2, local copies, waits for them, and re-layouts: none -> 10.6 us  [the longest x1 8.59 us: per_device(): out_full = jnp.concatenate(lax.all_to_all(jnp.stack([out_weight[0]] * lax...]
    all_to_all x0 -> x1, local copies, waits for them, and re-layouts: none -> 5.72 us  [per_device(): lax.all_to_all(jnp.stack([out_weight[0]] * lax.axis_size('seq')), 'seq',...]
    all_gather x1 -> x0, local copies, waits for them, and re-layouts: 4.65 us -> none  [per_device(): lax.all_gather(out_weight[0], 'seq', axis=0, tiled=True)]
    unnamed x57 -> x75, local copies, waits for them, and re-layouts: 12.9 us -> 12.9 us
  transfers between devices with their start and end apart: 7 -> 7, of which waited for: 7 -> 7; matrix products, arithmetic and copies ran while one was open for 9% -> 5% of each run, Pallas kernels for 0% -> 0%
where the time goes in v1:
time: 459 us; the launch traced here: 451 us
  waiting for transfers between devices  210 us (46%)
  blocking collectives  84.7 us (18%)
  local copies, waits for them, and re-layouts  53 us (12%)
  matrix products  39 us (8%)
  other arithmetic  34.5 us (8%)
  starting transfers between devices  15.1 us (3%)
  between operations  15.1 us (3%)
    reduce_scatter x2, waiting for transfers between devices, run(): lax.psum_scatter(jnp.einsum('sgpqe,dge->spqd', returned, out_full, prefer...  74.9 us
    all_to_all x1, waiting for transfers between devices, per_device(): lax.all_to_all(jnp.stack([out_weight[0]] * lax.axis_size('seq')), 'seq',...  66.6 us
    all_gather x2, waiting for transfers between devices, run(): mixed_rows = lax.all_gather(mixed_rows, 'cfg', axis=0, tiled=True)  48.5 us
    all_to_all x2, blocking collectives, run(): lax.all_to_all(attended, 'seq', split_axis=2, concat_axis=0, tiled=True)  32 us
    all_to_all x1, blocking collectives, run(): lax.all_to_all(outgoing, 'seq', split_axis=0, concat_axis=3, tiled=True)  30.6 us
    all_gather x1, blocking collectives, per_device(): lax.all_gather(predicted, ('section', 'cfg'), axis=0, tiled=True)  22.1 us
    all_to_all x1, waiting for transfers between devices, run(): lax.all_to_all(outgoing, 'seq', split_axis=0, concat_axis=3, tiled=True)  18.1 us
    dot_general x2, matrix products, run(): jnp.einsum('spqd,djge->sgjpqe', mixed_rows, qkv_full, preferred_element_t...  16.2 us
  transfers between devices with their start and end apart: 7, of which 7 were waited for; matrix products, arithmetic and copies ran while one was open for 5% of the time, Pallas kernels for 0%

profile of v1, /device:TPU:1, one launch (start us, length us, event | category | flops | bytes accessed | tf_op | source)
XLA Modules:
  0.0 451.0 jit_solution(5998155164784358680)
XLA Ops:
  7.3 1.4 fusion.93
  8.7 1.1 convert_reduce_fusion.1
  9.9 1.2 fusion.54
  11.2 2.0 fusion.60
  13.3 12.7 %copy.39 = bf16[1,3072,3,512]{1,3,2,0:T(8,128)(2,1)} copy(bf16[1,3072,3,512]{3,1,2,0:T(8,128)(2,1)} %param.15) | data formatting | bytes 18874368 | tf_op args[3]
  26.4 19.9 %all-gather.4.cloned.1.call-done = bf16[4,4,16,3072]{3,2,1,0:T(8,128)(2,1)} async-done(((bf16[1,4,16,3072]{3,2,1,0:T(8,128)(2,1)}), bf16[4,4,16,3072]{3,2,1,0:T(8,128)(2,1)}) %all-gather.4.cloned.1.call-update) | async-done | bytes 1572880 | tf_op jit(solution)/shard_map/all_gather | solution.py:120
  46.3 8.1 %convolution_bitcast_fusion.3 = f32[4,8,3,4,16,64]{5,4,1,2,3,0:T(8,128)S(1)} fusion(bf16[3072,3,8,64,1,1]{0,3,2,1,5,4:T(8,128)(2,1)} %bitcast.168, bf16[4,4,16,3072]{3,2,1,0:T(8,128)(2,1)} %all-gather.4.cloned.1.call-done), kind=kOutput, calls=%fused_computation.21 | convolution fusion | flops 2415919104 | bytes 12582912 | tf_op jit(solution)/shard_map/spqd,djge->sgjpqe/dot_general | solution.py:121
  55.2 1.3 multiply_reduce_fusion.3
  56.6 1.3 fusion.45
  60.7 1.5 copy.44
  62.2 10.0 %all-to-all-start = ((bf16[32,3,4,1024]{3,2,1,0:T(4,128)(2,1)}), bf16[32,3,4,1024]{3,2,1,0:T(4,128)(2,1)S(1)}, u32[]{:S(2)}, u32[]{:S(2)}) async-start(bf16[32,3,4,1024]{3,2,1,0:T(4,128)(2,1)} %copy.44), calls=%async_computation | async-start | bytes 1572864 | tf_op jit(solution)/shard_map/all_to_all | solution.py:128
  73.7 1.3 fusion.80
  75.1 18.1 %all-to-all-done = bf16[32,3,4,1024]{3,2,1,0:T(4,128)(2,1)S(1)} async-done(((bf16[32,3,4,1024]{3,2,1,0:T(4,128)(2,1)}), bf16[32,3,4,1024]{3,2,1,0:T(4,128)(2,1)S(1)}, u32[]{:S(2)}, u32[]{:S(2)}) %all-to-all-start) | async-done | bytes 786464 | tf_op jit(solution)/shard_map/all_to_all | solution.py:128
  95.7 2.5 fusion
  98.2 3.7 fusion.2
  101.9 4.0 fusion.27
  106.8 16.1 %all_to_all.65 = bf16[1,4,32,1024]{3,1,0,2:T(4,128)(2,1)} all-to-all(bf16[1,4,32,1024]{3,1,0,2:T(4,128)(2,1)S(1)} %copy.52), channel_id=1, replica_groups=mesh['section'=2,'seq'=32,'cfg'=4] {'seq'}, dimensions={2} | all-to-all | bytes 524288 | tf_op jit(solution)/shard_map/all_to_all | solution.py:150
  122.9 2.0 stack.29
  124.9 4.1 all-to-all-start.2
  129.0 2.1 reshape.448
  131.1 66.6 %all-to-all-done.2 = bf16[32,96,512]{2,1,0:T(8,128)(2,1)S(1)} async-done(((bf16[32,96,512]{2,1,0:T(8,128)(2,1)}), bf16[32,96,512]{2,1,0:T(8,128)(2,1)S(1)}, u32[]{:S(2)}, u32[]{:S(2)}) %all-to-all-start.2) | async-done | bytes 3145760 | tf_op jit(solution)/shard_map/all_to_all | solution.py:90
  197.7 5.7 %copy.54 = bf16[32,96,512]{1,0,2:T(8,128)(2,1)} copy(bf16[32,96,512]{2,1,0:T(8,128)(2,1)S(1)} %all-to-all-done.2) | data formatting | bytes 6291456 | tf_op jit(solution)/shard_map/all_to_all | solution.py:90
  203.4 8.6 %reshape.443 = bf16[3072,8,64,1,1]{0,2,1,3,4:T(8,128)(2,1)} reshape(bf16[32,96,512]{1,0,2:T(8,128)(2,1)} %copy.54) | data formatting | bytes 6291456 | tf_op jit(solution)/shard_map/reshape;reshape | solution.py:91
  212.0 4.8 %convolution_bitcast_fusion.1 = f32[4,4,16,3072]{3,2,1,0:T(8,128)} fusion(bf16[4,8,4,16,64]{4,3,2,1,0:T(8,128)(2,1)} %reshape.448, bf16[3072,8,64,1,1]{0,2,1,3,4:T(8,128)(2,1)} %reshape.443), kind=kOutput, calls=%fused_computation.15 | convolution fusion | flops 805306368 | bytes 6553600 | tf_op jit(solution)/shard_map/sgpqe,dge->spqd/dot_general | solution.py:153
  217.1 40.8 %reduce-scatter.3.cloned.1.call-done = f32[1,4,16,3072]{3,2,1,0:T(8,128)} async-done(((f32[4,4,16,3072]{3,2,1,0:T(8,128)}), f32[1,4,16,3072]{3,2,1,0:T(8,128)}) %reduce-scatter.3.cloned.1.call-update) | async-done | bytes 786448 | tf_op jit(solution)/shard_map/reduce_scatter | solution.py:152
  257.8 1.3 fusion.62
  259.9 1.3 collective-permute-done
  262.8 28.7 %all-gather.6.cloned.1.call-done = bf16[4,4,16,3072]{3,2,1,0:T(8,128)(2,1)} async-done(((bf16[1,4,16,3072]{3,2,1,0:T(8,128)(2,1)}), bf16[4,4,16,3072]{3,2,1,0:T(8,128)(2,1)}) %all-gather.6.cloned.1.call-update) | async-done | bytes 1572880 | tf_op jit(solution)/shard_map/all_gather | solution.py:120
  291.4 8.1 %convolution_bitcast_fusion.2 = f32[4,8,3,4,16,64]{5,4,1,3,0,2:T(8,128)S(1)} fusion(bf16[3072,3,8,64,1,1]{0,3,2,5,4,1:T(8,128)(2,1)} %bitcast.169, bf16[4,4,16,3072]{3,2,1,0:T(8,128)(2,1)} %all-gather.6.cloned.1.call-done), kind=kOutput, calls=%fused_computation.20 | convolution fusion | flops 2415919104 | bytes 12582912 | tf_op jit(solution)/shard_map/spqd,djge->sgjpqe/dot_general | solution.py:121
  301.1 1.3 multiply_reduce_fusion.1
  302.5 1.3 fusion.43
  305.0 1.0 stack.30
  306.7 1.1 copy.59
  308.1 1.0 pad_maximum_fusion.1
  309.8 30.6 %all_to_all.66 = bf16[32,3,4,1024]{3,2,1,0:T(4,128)(2,1)S(1)} all-to-all(bf16[32,3,4,1024]{3,2,1,0:T(4,128)(2,1)S(1)} %copy.60), channel_id=1, replica_groups=mesh['section'=2,'seq'=32,'cfg'=4] {'seq'}, dimensions={0} | all-to-all | bytes 1572864 | tf_op jit(solution)/shard_map/all_to_all | solution.py:128
  343.6 1.3 broadcast_select_fusion
  344.9 1.7 copy.61
  346.6 1.3 squeeze.79
  348.0 2.5 fusion.1
  350.5 3.7 fusion.4
  354.2 4.0 fusion.37
  359.2 16.0 %all_to_all.67 = bf16[1,4,32,1024]{3,1,0,2:T(4,128)(2,1)S(1)} all-to-all(bf16[1,4,32,1024]{3,1,0,2:T(4,128)(2,1)S(1)} %copy.67), channel_id=1, replica_groups=mesh['section'=2,'seq'=32,'cfg'=4] {'seq'}, dimensions={2} | all-to-all | bytes 524288 | tf_op jit(solution)/shard_map/all_to_all | solution.py:150
  375.5 4.6 %convolution_bitcast_fusion = f32[4,4,16,3072]{3,2,1,0:T(8,128)} fusion(bf16[4,8,4,16,64]{4,3,2,1,0:T(8,128)(2,1)S(1)} %reshape.450, bf16[3072,8,64,1,1]{0,2,1,3,4:T(8,128)(2,1)} %reshape.443), kind=kOutput, calls=%fused_computation.14 | convolution fusion | flops 805306368 | bytes 6553600 | tf_op jit(solution)/shard_map/sgpqe,dge->spqd/dot_general | solution.py:153
  382.1 1.4 maximum_select_fusion
  383.5 34.1 %reduce-scatter.5.cloned.1.call-done = f32[1,4,16,3072]{3,2,1,0:T(8,128)} async-done(((f32[4,4,16,3072]{3,2,1,0:T(8,128)}), f32[1,4,16,3072]{3,2,1,0:T(8,128)}) %reduce-scatter.5.cloned.1.call-update) | async-done | bytes 786448 | tf_op jit(solution)/shard_map/reduce_scatter | solution.py:152
  417.6 1.4 convert_reduce_fusion.2
  419.7 22.1 %all-gather = f32[32,16,64]{2,1,0:T(8,128)S(1)} all-gather(f32[4,16,64]{2,1,0:T(8,128)S(1)} %fusion.65), channel_id=2, replica_groups=mesh['section'=2,'seq'=32,'cfg'=4] {'section','cfg'}, dimensions={0}, use_global_device_ids=true | all-gather | bytes 147456 | tf_op jit(solution)/shard_map/all_gather | solution.py:170
  441.8 2.4 fusion.77
  (170 shorter events, 22.5 us)
Async XLA Ops:
  7.2 412.2 %copy-start = (bf16[3072,64]{0,1:T(8,128)(2,1)S(1)}, bf16[3072,64]{0,1:T(8,128)(2,1)}, u32[]{:S(2)}) copy-start(bf16[3072,64]{0,1:T(8,128)(2,1)} %param.19) | copy-start | bytes 1179652
  7.2 39.1 %all-gather.4.cloned.1.call-start = ((), (), s32[]{:S(2)}) async-start(), calls=%async_computation.7 | async-start | bytes 1966080 | tf_op jit(solution)/shard_map/all_gather | solution.py:120
  7.3 18.7 %copy-start.31 = (pred[4,16]{1,0:T(4,128)(4,1)}, pred[4,16]{1,0:T(4,128)(4,1)S(1)}, u32[]{:S(2)}) copy-start(pred[4,16]{1,0:T(4,128)(4,1)S(1)} %add_compare_fusion.1) | copy-start | bytes 196
  8.7 2.4 copy-start.18
  8.7 2.4 copy-start.20
  8.7 2.4 copy-start.22
  8.7 2.4 copy-start.24
  13.2 12.8 %copy-start.33 = (s32[3,2,4,16]{3,2,1,0:T(4,128)S(1)}, s32[3,2,4,16]{3,2,1,0:T(4,128)}, u32[]{:S(2)}) copy-start(s32[3,2,4,16]{3,2,1,0:T(4,128)} %param.23) | copy-start | bytes 4612
  57.9 1.2 copy-start.12
  57.9 1.2 copy-start.14
  57.9 14.3 %copy-start.16 = (bf16[1,1,1,2048,128]{4,3,2,1,0:T(8,128)(2,1)S(1)}, bf16[1,1,1,2048,128]{4,3,2,1,0:T(8,128)(2,1)}, u32[]{:S(2)}) copy-start(bf16[1,1,1,2048,128]{4,3,2,1,0:T(8,128)(2,1)} %param.14) | copy-start | bytes 1572868
  58.7 13.7 %copy-start.35 = (s32[2]{0:T(128)S(1)}, s32[2]{0:T(128)}, u32[]{:S(2)}) copy-start(s32[2]{0:T(128)} %param.21) | copy-start | bytes 28
  58.8 14.3 %copy-start.36 = (s32[4]{0:T(128)S(1)}, s32[4]{0:T(128)}, u32[]{:S(2)}) copy-start(s32[4]{0:T(128)} %param.22) | copy-start | bytes 52
  62.2 31.1 %all-to-all-start = ((bf16[32,3,4,1024]{3,2,1,0:T(4,128)(2,1)}), bf16[32,3,4,1024]{3,2,1,0:T(4,128)(2,1)S(1)}, u32[]{:S(2)}, u32[]{:S(2)}) async-start(bf16[32,3,4,1024]{3,2,1,0:T(4,128)(2,1)} %copy.44), calls=%async_computation | async-start | bytes 1572864 | tf_op jit(solution)/shard_map/all_to_all | solution.py:128
  72.4 25.8 %copy-start.2 = (bf16[2048,128]{0,1:T(8,128)(2,1)}, bf16[2048,128]{0,1:T(8,128)(2,1)S(1)}, u32[]{:S(2)}) copy-start(bf16[2048,128]{0,1:T(8,128)(2,1)S(1)} %copy.49) | copy-start | bytes 1572868
  75.1 23.1 %copy-start.27 = (pred[4,2048]{1,0:T(4,128)(4,1)}, pred[4,2048]{1,0:T(4,128)(4,1)S(1)}, u32[]{:S(2)}) copy-start(pred[4,2048]{1,0:T(4,128)(4,1)S(1)} %iota_compare_fusion) | copy-start | bytes 24580
  93.6 1.3 copy-start.4
  94.0 0.9 copy-start.6
  101.9 21.0 %copy-start.26 = (bf16[1,96,512]{2,1,0:T(8,128)(2,1)S(1)}, bf16[1,96,512]{2,1,0:T(8,128)(2,1)}, u32[]{:S(2)}) copy-start(bf16[1,96,512]{2,1,0:T(8,128)(2,1)} %param.16) | copy-start | bytes 294916
  124.9 72.8 %all-to-all-start.2 = ((bf16[32,96,512]{2,1,0:T(8,128)(2,1)}), bf16[32,96,512]{2,1,0:T(8,128)(2,1)S(1)}, u32[]{:S(2)}, u32[]{:S(2)}) async-start(bf16[32,96,512]{2,1,0:T(8,128)(2,1)} %stack.29), calls=%async_computation.2 | async-start | bytes 6291456 | tf_op jit(solution)/shard_map/all_to_all | solution.py:90
  129.0 128.9 %reduce-scatter.3.cloned.1.call-start = ((), (), s32[]{:S(2)}) async-start(), calls=%async_computation.8 | async-start | bytes 3932160 | tf_op jit(solution)/shard_map/reduce_scatter | solution.py:152
  203.4 54.4 %copy-start.1 = (bf16[1,4,16,3072]{3,2,1,0:T(8,128)(2,1)S(1)}, bf16[1,4,16,3072]{3,2,1,0:T(8,128)(2,1)}, u32[]{:S(2)}) copy-start(bf16[1,4,16,3072]{3,2,1,0:T(8,128)(2,1)} %param.12) | copy-start | bytes 1179652
  203.4 54.4 %copy-start.17 = (f32[1,1,3072]{2,0,1:T(1,128)S(1)}, f32[1,1,3072]{2,0,1:T(1,128)}, u32[]{:S(2)}) copy-start(f32[1,1,3072]{2,0,1:T(1,128)} %get-tuple-element.35) | copy-start | bytes 36868
  203.4 54.4 %copy-start.32 = (pred[4,16]{1,0:T(4,128)(4,1)S(1)}, pred[4,16]{1,0:T(4,128)(4,1)}, u32[]{:S(2)}) copy-start(pred[4,16]{1,0:T(4,128)(4,1)} %copy-done.31) | copy-start | bytes 196
  212.0 49.6 %copy-start.19 = (f32[1,1,3072]{2,0,1:T(1,128)S(1)}, f32[1,1,3072]{2,0,1:T(1,128)}, u32[]{:S(2)}) copy-start(f32[1,1,3072]{2,0,1:T(1,128)} %copy-done.18) | copy-start | bytes 36868
  212.0 49.6 %copy-start.21 = (f32[1,1,3072]{2,0,1:T(1,128)S(1)}, f32[1,1,3072]{2,0,1:T(1,128)}, u32[]{:S(2)}) copy-start(f32[1,1,3072]{2,0,1:T(1,128)} %copy-done.20) | copy-start | bytes 36868
  212.0 49.6 %copy-start.23 = (f32[1,1,3072]{2,0,1:T(1,128)S(1)}, f32[1,1,3072]{2,0,1:T(1,128)}, u32[]{:S(2)}) copy-start(f32[1,1,3072]{2,0,1:T(1,128)} %copy-done.22) | copy-start | bytes 36868
  212.0 49.6 %copy-start.25 = (f32[1,1,3072]{2,0,1:T(1,128)S(1)}, f32[1,1,3072]{2,0,1:T(1,128)}, u32[]{:S(2)}) copy-start(f32[1,1,3072]{2,0,1:T(1,128)} %copy-done.24) | copy-start | bytes 36868
  216.8 74.6 %all-gather.6.cloned.1.call-start = ((), (), s32[]{:S(2)}) async-start(), calls=%async_computation.9 | async-start | bytes 1966080 | tf_op jit(solution)/shard_map/all_gather | solution.py:120
  259.2 2.1 collective-permute-start
  262.7 154.9 %reduce-scatter.5.cloned.1.call-start = ((), (), s32[]{:S(2)}) async-start(), calls=%async_computation.10 | async-start | bytes 3932160 | tf_op jit(solution)/shard_map/reduce_scatter | solution.py:152
  299.6 4.2 copy-start.13
  299.6 4.2 copy-start.15
  306.0 37.6 %copy-start.3 = (bf16[2048,128]{0,1:T(8,128)(2,1)S(1)}, bf16[2048,128]{0,1:T(8,128)(2,1)}, u32[]{:S(2)}) copy-start(bf16[2048,128]{0,1:T(8,128)(2,1)} %copy-done.2) | copy-start | bytes 1572868
  306.0 37.6 %copy-start.28 = (pred[4,2048]{1,0:T(4,128)(4,1)S(1)}, pred[4,2048]{1,0:T(4,128)(4,1)}, u32[]{:S(2)}) copy-start(pred[4,2048]{1,0:T(4,128)(4,1)} %copy-done.27) | copy-start | bytes 24580
  341.5 1.1 copy-start.8
  341.6 1.0 copy-start.10
  358.3 21.8 %copy-start.34 = (f32[1,3]{1,0:T(1,128)S(1)}, f32[1,3]{1,0:T(1,128)}, u32[]{:S(2)}) copy-start(f32[1,3]{1,0:T(1,128)} %param.20) | copy-start | bytes 40
  358.3 22.4 %copy-start.30 = (f32[2,3072]{1,0:T(2,128)S(1)}, f32[2,3072]{1,0:T(2,128)}, u32[]{:S(2)}) copy-start(f32[2,3072]{1,0:T(2,128)} %param.18) | copy-start | bytes 73732
  358.3 22.4 %copy-start.5 = (bf16[1,1,4,32,1024]{4,3,2,1,0:T(8,128)(2,1)S(1)}, bf16[1,1,4,32,1024]{4,3,2,1,0:T(8,128)(2,1)}, u32[]{:S(2)}) copy-start(bf16[1,1,4,32,1024]{4,3,2,1,0:T(8,128)(2,1)} %copy-done.4) | copy-start | bytes 786436
  358.3 22.8 %copy-start.7 = (bf16[1,1,4,32,1024]{4,3,2,1,0:T(8,128)(2,1)S(1)}, bf16[1,1,4,32,1024]{4,3,2,1,0:T(8,128)(2,1)}, u32[]{:S(2)}) copy-start(bf16[1,1,4,32,1024]{4,3,2,1,0:T(8,128)(2,1)} %copy-done.6) | copy-start | bytes 786436
  358.3 23.1 %copy-start.9 = (bf16[1,1,4,32,1024]{4,3,2,1,0:T(8,128)(2,1)S(1)}, bf16[1,1,4,32,1024]{4,3,2,1,0:T(8,128)(2,1)}, u32[]{:S(2)}) copy-start(bf16[1,1,4,32,1024]{4,3,2,1,0:T(8,128)(2,1)} %copy-done.8) | copy-start | bytes 786436
  358.3 23.5 %copy-start.11 = (bf16[1,1,4,32,1024]{4,3,2,1,0:T(8,128)(2,1)S(1)}, bf16[1,1,4,32,1024]{4,3,2,1,0:T(8,128)(2,1)}, u32[]{:S(2)}) copy-start(bf16[1,1,4,32,1024]{4,3,2,1,0:T(8,128)(2,1)} %copy-done.10) | copy-start | bytes 786436
  380.1 61.7 %copy-start.29 = (f32[1,4,16,64]{3,2,1,0:T(8,128)S(1)}, f32[1,4,16,64]{3,2,1,0:T(8,128)}, u32[]{:S(2)}) copy-start(f32[1,4,16,64]{3,2,1,0:T(8,128)} %param.13) | copy-start | bytes 49156
Sparse Core Ops, SparseCore 0:
  13.4 32.8 all-gather.3
  217.0 40.8 reduce-scatter.2
  262.9 28.5 all-gather.5
  380.2 37.3 reduce-scatter.4
